TPU v7x, 32 devices: a whole 2x2x4 slice. The times are simulated.
32 devices in a mesh: group: 2 (over x), strip: 16 (over z, y, core).
Axes of the slice: x: 2, y: 2, z: 4, core: 2. Of those that a mesh axis runs over, the one named last changes fastest.
Arguments:
- strip_fields: float32 [3, 64, 128, 128], P(None, ('group', 'strip')), may hold values from -18 to 18
- strip_riser: int32 [64, 1], P('group'), may hold values from 0 to 3; in each aligned block of 2 rows (0 to 1, 2 to 3, ...) at most 2 rows name the same one
- strip_node: int32 [64], P('group'), may hold values from 0 to 1023
- riser_owner: int32 [2, 4], P('group'), may hold values from 0 to 15, as said below
- pivot_inv: float32 [32, 8, 128, 128], P(('group', 'strip')), may hold values from -0.2 to 1
- lower_block: float32 [32, 7, 128, 128], P(('group', 'strip')), may hold values from -0.109375 to 0.109375
- upper_block: float32 [32, 7, 128, 128], P(('group', 'strip')), may hold values from -0.109375 to 0.109375
Outputs:
- vorticity: float32 [64, 128, 128], P(('group', 'strip'))
- displacement: float32 [32, 16, 1024], P(('group', 'strip'))
Inputs may be any that keep to these rules, and one draw needn't show every extreme that they name: `strip_riser`: in each aligned block of 2 strips (the strips of one device) no riser is named more than 2 times, and some block names one riser exactly 2 times. `riser_owner`: the 4 owners in a row are distinct devices.
All inputs are finite; a program needn't handle non-finite values.
Results may differ from a plain program's by a relative error of at most 0.0003.
Values sent between devices are 32-bit elements; how exact they have to be, the bound alone decides.
No kernel may reach another device: no remote copies, remote signals or barrier semaphores. Data moves between devices by JAX's collectives and lax.ppermute only.
A program may use at most 64 MiB of HBM per device.

v0:
```python
import jax
import jax.numpy as jnp
from jax import lax
from jax.sharding import PartitionSpec as P

NSUB = 8
COUPLED = 2
TIME_STEP = 0.25
VISCOSITY = 0.05
COUPLING = 0.5
EXACT_DOT = lax.Precision.HIGHEST


def make_kernels(grid_cells):
    centre = jnp.arange(grid_cells, dtype=jnp.float32) - grid_cells / 2.0 + 0.5
    near_x = (centre / (grid_cells / 16.0))[None, :]
    near_y = (centre / (grid_cells / 16.0))[:, None]
    bell_near = jnp.exp(-(near_x * near_x + near_y * near_y) / 2.0)
    source_x = -near_x * bell_near
    source_y = -near_y * bell_near
    wide_x = (centre / (grid_cells / 8.0))[None, :]
    wide_y = (centre / (grid_cells / 8.0))[:, None]
    bell_wide = jnp.exp(-(wide_x * wide_x + wide_y * wide_y) / 2.0)
    lift_kernel = -wide_x * bell_wide
    drag_kernel = wide_y * bell_wide
    lift_kernel = lift_kernel / jnp.sqrt(jnp.sum(lift_kernel * lift_kernel))
    drag_kernel = drag_kernel / jnp.sqrt(jnp.sum(drag_kernel * drag_kernel))
    return (source_x, source_y, lift_kernel, drag_kernel)


def strip_step(vorticity, flow_x, flow_y, motion, kernels, substeps):
    source_x, source_y, lift_kernel, drag_kernel = kernels
    halves = motion.reshape(motion.shape[0], 2, substeps)
    earlier = jnp.concatenate([jnp.zeros_like(halves[:, :, :1]), halves[:, :, :-1]], axis=2)
    velocity = halves - earlier
    lift_rows = []
    drag_rows = []
    for substep in range(substeps):
        right_cell = jnp.roll(vorticity, -1, axis=2)
        left_cell = jnp.roll(vorticity, 1, axis=2)
        upper_cell = jnp.roll(vorticity, -1, axis=1)
        lower_cell = jnp.roll(vorticity, 1, axis=1)
        laplacian = right_cell + left_cell + upper_cell + lower_cell - 4.0 * vorticity
        tendency = (
            VISCOSITY * laplacian
            - flow_x * (0.5 * (right_cell - left_cell))
            - flow_y * (0.5 * (upper_cell - lower_cell))
        )
        forcing = (
            velocity[:, 0, substep][:, None, None] * source_x
            - velocity[:, 1, substep][:, None, None] * source_y
        )
        vorticity = vorticity + TIME_STEP * tendency + COUPLING * forcing
        lift_rows.append(jnp.sum(vorticity * lift_kernel, axis=(1, 2)))
        drag_rows.append(jnp.sum(vorticity * drag_kernel, axis=(1, 2)))
    return (vorticity, jnp.stack(lift_rows + drag_rows, axis=1))


def apply_block(vectors, matrix):
    return lax.dot_general(vectors, matrix, (((1,), (1,)), ((), ())), precision=EXACT_DOT)


def first_contract(left_side, right_side):
    return lax.dot_general(left_side, right_side, (((0,), (0,)), ((), ())), precision=EXACT_DOT)


def beam_solve(beam_load, pivot_inv, lower_block, upper_block):
    block_count = pivot_inv.shape[0]
    block_size = pivot_inv.shape[1]
    blocks = beam_load.reshape(beam_load.shape[0], block_count, block_size)
    carried = [blocks[:, 0]]
    for block_index in range(1, block_count):
        pivoted = apply_block(carried[-1], pivot_inv[block_index - 1])
        carried.append(blocks[:, block_index] - apply_block(pivoted, lower_block[block_index - 1]))
    solved = [apply_block(carried[-1], pivot_inv[block_count - 1])]
    for block_index in range(block_count - 2, -1, -1):
        remainder = carried[block_index] - apply_block(solved[0], upper_block[block_index])
        solved.insert(0, apply_block(remainder, pivot_inv[block_index]))
    return jnp.concatenate(solved, axis=1)


def local(strip_fields, strip_riser, strip_node, riser_owner, pivot_inv, lower_block, upper_block):
    devices = lax.axis_size("strip")
    position = lax.axis_index("strip")
    per_device = strip_fields.shape[1]
    grid_cells = strip_fields.shape[2]
    node_count = pivot_inv.shape[1] * pivot_inv.shape[2]
    riser_count = riser_owner.shape[1]
    substeps = NSUB
    total_strips = per_device * devices * lax.axis_size("group")
    kernels = make_kernels(grid_cells)
    riser_match = (
        strip_riser[:, 0][:, None] == jnp.arange(riser_count, dtype=jnp.int32)[None, :]
    ).astype(jnp.int32)
    owner_index = jnp.sum(riser_match * riser_owner[0][None, :], axis=1)
    owned_here = owner_index == position
    node_hit = (
        owned_here[:, None]
        & (strip_node[:, None] == jnp.arange(node_count, dtype=jnp.int32)[None, :])
    ).astype(jnp.float32)
    local_owner = lax.dynamic_slice_in_dim(owner_index, position * per_device, per_device)
    local_node = lax.dynamic_slice_in_dim(strip_node, position * per_device, per_device)
    top_taper = 1.0 - jnp.arange(node_count, dtype=jnp.float32) / node_count
    vorticity = strip_fields[0]
    flow_x = strip_fields[1]
    flow_y = strip_fields[2]
    motion = jnp.zeros((per_device, 2 * substeps), jnp.float32)
    displacement = jnp.zeros((2 * substeps, node_count), jnp.float32)
    for coupled_step in range(COUPLED):
        vorticity, force_rows = strip_step(vorticity, flow_x, flow_y, motion, kernels, substeps)
        partial_drag = jnp.sum(force_rows[:, substeps:], axis=0)
        total_drag = lax.psum(partial_drag, ("group", "strip"))
        offset = total_drag / jnp.sqrt(jnp.float32(total_strips))
        beam_load = first_contract(
            lax.all_gather(force_rows, "strip", axis=0, tiled=True), node_hit
        )
        displacement = beam_solve(beam_load, pivot_inv[0], lower_block[0], upper_block[0])
        displacement = displacement.at[substeps:, :].add(offset[:, None] * top_taper[None, :])
        if coupled_step + 1 < COUPLED:
            every_owner = lax.all_gather(displacement[None], "strip", axis=0, tiled=True)
            chosen = jnp.take(every_owner, local_owner, axis=0)
            node_pick = jnp.broadcast_to(local_node[:, None, None], (per_device, 2 * substeps, 1))
            motion = jnp.take_along_axis(chosen, node_pick, axis=2)[:, :, 0]
    return (vorticity, displacement[None])


def solution(mesh):
    in_specs = (
        P(None, ("group", "strip"), None, None),
        P("group", None),
        P("group"),
        P("group", None),
        P(("group", "strip"), None, None, None),
        P(("group", "strip"), None, None, None),
        P(("group", "strip"), None, None, None),
    )
    out_specs = (P(("group", "strip"), None, None), P(("group", "strip"), None, None))
    return jax.shard_map(local, mesh=mesh, in_specs=in_specs, out_specs=out_specs, check_vma=False)
```

profile of v0, /device:TPU:0, one launch (start us, length us, event | category | flops | bytes accessed | tf_op | source)
XLA Modules:
  0.0 231.5 jit_solution(9136430588047142506)
XLA Ops:
  7.2 0.9 slice_bitcast_fusion
  8.5 0.8 copy-done
  12.4 0.7 multiply_reduce_fusion.32
  14.6 0.5 multiply_reduce_fusion.23
  15.9 42.0 %psum.14 = f32[8]{0:T(128)S(1)} all-reduce(f32[8]{0:T(128)S(1)} %reduce_sum.352), channel_id=1, replica_groups=mesh['group'=2,'strip'=16] {'group','strip'}, use_global_device_ids=true, to_apply=%region_20.21 | all-reduce | flops 8 | bytes 64 | tf_op jit(solution)/shard_map/psum | solution.py:112
  58.8 21.0 %all-gather = f32[16,2,16]{2,1,0:T(2,128)S(1)} all-gather(f32[1,2,16]{2,1,0:T(2,128)S(1)} %bitcast.564), channel_id=1, replica_groups=mesh['group'=2,'strip'=16] {'strip'}, dimensions={0}, use_global_device_ids=true | all-gather | bytes 2176 | tf_op jit(solution)/shard_map/all_gather | solution.py:115
  79.8 0.7 copy-done.6
  80.5 0.7 copy-done.5
  81.5 1.0 fusion.167
  82.5 1.1 convolution_subtract_fusion.27
  83.6 1.1 fusion.159
  84.7 1.1 convolution_subtract_fusion.26
  85.8 1.1 fusion.149
  86.9 1.1 convolution_subtract_fusion.25
  88.0 1.1 fusion.139
  89.0 1.1 convolution_subtract_fusion.24
  90.1 1.1 fusion.129
  91.2 1.1 convolution_subtract_fusion.23
  92.2 1.1 fusion.119
  93.3 1.1 convolution_subtract_fusion.22
  94.3 1.1 fusion.109
  95.4 1.1 convolution_subtract_fusion.21
  96.5 1.1 fusion.99
  99.3 0.3 convolution_subtract_fusion.16
  100.2 0.3 convolution_subtract_fusion.14
  100.9 0.6 copy-done.3
  102.2 33.8 %all-gather.4.cloned.1.call-done = f32[16,16,1024]{2,1,0:T(8,128)} async-done(((f32[1,16,1024]{2,1,0:T(8,128)}), f32[16,16,1024]{2,1,0:T(8,128)}) %all-gather.4.cloned.1.call-update) | async-done | bytes 1048592 | tf_op jit(solution)/shard_map/all_gather | solution.py:120
  136.0 1.8 gather_fusion
  137.8 0.8 gather_fusion.1
  142.2 1.1 multiply_reduce_fusion.7
  144.2 38.9 %psum.15 = f32[8]{0:T(128)S(1)} all-reduce(f32[8]{0:T(128)S(1)} %reduce_sum.369), channel_id=1, replica_groups=mesh['group'=2,'strip'=16] {'group','strip'}, use_global_device_ids=true, to_apply=%region_38.39 | all-reduce | flops 8 | bytes 64 | tf_op jit(solution)/shard_map/psum | solution.py:112
  183.9 20.6 %all-gather.1 = f32[16,2,16]{2,1,0:T(2,128)S(1)} all-gather(f32[1,2,16]{2,1,0:T(2,128)S(1)} %bitcast.565), channel_id=1, replica_groups=mesh['group'=2,'strip'=16] {'strip'}, dimensions={0}, use_global_device_ids=true | all-gather | bytes 2176 | tf_op jit(solution)/shard_map/all_gather | solution.py:115
  204.8 1.0 fusion.164
  205.8 1.1 convolution_subtract_fusion.13
  206.9 1.1 fusion.155
  208.0 1.1 convolution_subtract_fusion.12
  209.0 1.1 fusion.145
  210.1 1.1 convolution_subtract_fusion.11
  211.2 1.1 fusion.135
  212.2 1.1 convolution_subtract_fusion.10
  213.3 1.1 fusion.125
  214.3 1.1 convolution_subtract_fusion.9
  215.4 1.1 fusion.115
  216.5 1.1 convolution_subtract_fusion.8
  217.5 1.1 fusion.105
  218.6 1.1 convolution_subtract_fusion.7
  219.6 1.1 fusion.97
  224.1 0.6 copy-done.4
  (204 shorter events, 17.4 us)
Async XLA Ops:
  7.2 128.8 %all-gather.4.cloned.1.call-start = ((), (), s32[]{:S(2)}) async-start(), calls=%async_computation | async-start | bytes 1114112 | tf_op jit(solution)/shard_map/all_gather | solution.py:120
  8.3 1.0 copy-start
  79.8 0.7 copy-start.6
  79.8 0.7 copy-start.7
  80.5 0.7 copy-start.5
  84.7 12.9 %copy-start.2 = (f32[1,7,128,128]{3,2,1,0:T(8,128)S(1)}, f32[1,7,128,128]{3,2,1,0:T(8,128)}, u32[]{:S(2)}) copy-start(f32[1,7,128,128]{3,2,1,0:T(8,128)} %param.17) | copy-start | bytes 1376260
  85.8 12.0 %copy-start.1 = (f32[1,8,128,128]{3,2,1,0:T(8,128)S(1)}, f32[1,8,128,128]{3,2,1,0:T(8,128)}, u32[]{:S(2)}) copy-start(f32[1,8,128,128]{3,2,1,0:T(8,128)} %param.15) | copy-start | bytes 1572868
  100.9 0.6 copy-start.3
  224.1 0.6 copy-start.4
Sparse Core Ops, SparseCore 0:
  101.7 34.2 all-gather.3
where the time goes:
time: 233 us; the launch traced here: 232 us
  blocking collectives  123 us (53%)
  matrix products  38.5 us (17%)
  waiting for transfers between devices  33.8 us (15%)
  between operations  16.3 us (7%)
  local copies, waits for them, and re-layouts  14.4 us (6%)
  other arithmetic  5.94 us (3%)
    psum x2, blocking collectives, local(): total_drag = lax.psum(partial_drag, ('group', 'strip'))  80.9 us
    all_gather x2, blocking collectives, local(): lax.all_gather(force_rows, 'strip', axis=0, tiled=True)  41.6 us
    dot_general x58, matrix products, apply_block(): lax.dot_general(vectors, matrix, (((1,), (1,)), ((), ())), precision=EXAC...  38 us
    all_gather x1, waiting for transfers between devices, local(): lax.all_gather(displacement[None], 'strip', axis=0, tiled=True)  33.8 us
  transfers between devices with their start and end apart: 1, of which 1 were waited for; matrix products, arithmetic and copies ran while one was open for 0% of the time, Pallas kernels for 0%

commit v1 on v0

--- a/solution.py
+++ b/solution.py
@@ -9,6 +9,28 @@
 VISCOSITY = 0.05
 COUPLING = 0.5
 EXACT_DOT = lax.Precision.HIGHEST
+
+
+def in_order(blocks, dim):
+    blocks = jnp.moveaxis(blocks, 0, dim)
+    lengths = blocks.shape
+    return blocks.reshape(*lengths[:dim], lengths[dim] * lengths[dim + 1], *lengths[dim + 2 :])
+
+
+def doubled(value, axis):
+    size = lax.axis_size(axis)
+    blocks = value[None]
+    for level in range(size.bit_length() - 1):
+        distance = 1 << level
+        partner_block = lax.ppermute(blocks, axis, [(i, i ^ distance) for i in range(size)])
+        both = jnp.stack([blocks, partner_block])
+        upper = lax.axis_index(axis) >> level & 1
+        blocks = jnp.where(upper == 0, both, both[::-1]).reshape(-1, *value.shape)
+    return blocks
+
+
+def doubled_up(x, axis, dim):
+    return in_order(doubled(x, axis), dim)
 
 
 def make_kernels(grid_cells):
@@ -111,9 +133,7 @@
         partial_drag = jnp.sum(force_rows[:, substeps:], axis=0)
         total_drag = lax.psum(partial_drag, ("group", "strip"))
         offset = total_drag / jnp.sqrt(jnp.float32(total_strips))
-        beam_load = first_contract(
-            lax.all_gather(force_rows, "strip", axis=0, tiled=True), node_hit
-        )
+        beam_load = first_contract(doubled_up(force_rows, "strip", 0), node_hit)
         displacement = beam_solve(beam_load, pivot_inv[0], lower_block[0], upper_block[0])
         displacement = displacement.at[substeps:, :].add(offset[:, None] * top_taper[None, :])
         if coupled_step + 1 < COUPLED:

time: 233 us -> 190 us (0.82)
  blocking collectives: 123 us -> 81 us
  matrix products: 38.5 us -> 13.4 us
  waiting for transfers between devices: 33.8 us -> 50.1 us
  starting transfers between devices: 0.04 us -> 9.73 us
    all_gather x2 -> x0, blocking collectives: 41.6 us -> none  [local(): lax.all_gather(force_rows, 'strip', axis=0, tiled=True)]
    dot_general x58, matrix products: 38 us -> 12.9 us  [apply_block(): lax.dot_general(vectors, matrix, (((1,), (1,)), ((), ())), precision=EXAC...]
    ppermute x0 -> x8, waiting for transfers between devices: none -> 13 us  [doubled(): lax.ppermute(blocks, axis, [(i, i ^ distance) for i in range(size)])]
    ppermute x0 -> x8, starting transfers between devices: none -> 9.69 us  [doubled(): lax.ppermute(blocks, axis, [(i, i ^ distance) for i in range(size)])]
    all_gather x1, waiting for transfers between devices: 33.8 us -> 37 us  [local(): lax.all_gather(displacement[None], 'strip', axis=0, tiled=True)]
  transfers between devices with their start and end apart: 1 -> 9, of which waited for: 1 -> 7; matrix products, arithmetic and copies ran while one was open for 0% -> 0% of each run, Pallas kernels for 0% -> 0%
where the time goes in v1:
time: 190 us; the launch traced here: 189 us
  blocking collectives  81 us (43%)
  waiting for transfers between devices  50.1 us (26%)
  between operations  16.3 us (9%)
  matrix products  13.4 us (7%)
  local copies, waits for them, and re-layouts  12.9 us (7%)
  starting transfers between devices  9.73 us (5%)
  other arithmetic  5.99 us (3%)
    psum x2, blocking collectives, local(): total_drag = lax.psum(partial_drag, ('group', 'strip'))  81 us
    all_gather x1, waiting for transfers between devices, local(): lax.all_gather(displacement[None], 'strip', axis=0, tiled=True)  37 us
    ppermute x8, waiting for transfers between devices, doubled(): lax.ppermute(blocks, axis, [(i, i ^ distance) for i in range(size)])  13 us
    dot_general x58, matrix products, apply_block(): lax.dot_general(vectors, matrix, (((1,), (1,)), ((), ())), precision=EXAC...  12.9 us
    ppermute x8, starting transfers between devices, doubled(): lax.ppermute(blocks, axis, [(i, i ^ distance) for i in range(size)])  9.69 us
  transfers between devices with their start and end apart: 9, of which 7 were waited for; matrix products, arithmetic and copies ran while one was open for 0% of the time, Pallas kernels for 0%

profile of v1, /device:TPU:0, one launch (start us, length us, event | category | flops | bytes accessed | tf_op | source)
XLA Modules:
  0.0 189.5 jit_solution(10542166249154968222)
XLA Ops:
  7.2 0.9 slice_bitcast_fusion
  8.5 0.8 copy-done
  12.3 0.7 multiply_reduce_fusion.32
  14.6 0.5 multiply_reduce_fusion.23
  16.6 0.5 collective-permute-start
  17.3 41.6 %psum.14 = f32[8]{0:T(128)S(1)} all-reduce(f32[8]{0:T(128)S(1)} %reduce_sum.352), channel_id=1, replica_groups=mesh['group'=2,'strip'=16] {'group','strip'}, use_global_device_ids=true, to_apply=%region_20.21 | all-reduce | flops 8 | bytes 64 | tf_op jit(solution)/shard_map/psum | solution.py:134
  59.0 2.3 %collective-permute-start.1 = (f32[2,2,16]{2,1,0:T(2,128)S(1)}, f32[2,2,16]{2,1,0:T(2,128)S(1)}, u32[]{:S(2)}, u32[]{:S(2)}) collective-permute-start(f32[2,2,16]{2,1,0:T(2,128)S(1)} %get-tuple-element.325), channel_id=1, source_target_pairs={{0,2},{1,3},{2,0},{3,1},{4,6},{5,7},{6,4},{7,5},{8,10},{9,11},{10,... | collective-permute-start | bytes 776 | tf_op jit(solution)/shard_map/ppermute | solution.py:25
  61.3 1.6 collective-permute-done.1
  62.9 1.6 collective-permute-start.2
  64.5 2.1 %collective-permute-done.2 = f32[4,2,16]{2,1,0:T(2,128)S(1)} collective-permute-done((f32[4,2,16]{2,1,0:T(2,128)S(1)}, f32[4,2,16]{2,1,0:T(2,128)S(1)}, u32[]{:S(2)}, u32[]{:S(2)}) %collective-permute-start.2) | collective-permute-done | bytes 544 | tf_op jit(solution)/shard_map/ppermute | solution.py:25
  66.6 2.4 %collective-permute-start.3 = (f32[8,2,16]{2,1,0:T(2,128)S(1)}, f32[8,2,16]{2,1,0:T(2,128)S(1)}, u32[]{:S(2)}, u32[]{:S(2)}) collective-permute-start(f32[8,2,16]{2,1,0:T(2,128)S(1)} %bitcast.581), channel_id=1, source_target_pairs={{0,8},{1,9},{2,10},{3,11},{4,12},{5,13},{6,14},{7,15},{8,0},{9,1},... | collective-permute-start | bytes 3080 | tf_op jit(solution)/shard_map/ppermute | solution.py:25
  69.0 2.2 %collective-permute-done.3 = f32[8,2,16]{2,1,0:T(2,128)S(1)} collective-permute-done((f32[8,2,16]{2,1,0:T(2,128)S(1)}, f32[8,2,16]{2,1,0:T(2,128)S(1)}, u32[]{:S(2)}, u32[]{:S(2)}) %collective-permute-start.3) | collective-permute-done | bytes 1056 | tf_op jit(solution)/shard_map/ppermute | solution.py:25
  71.2 0.2 fusion.81
  72.1 0.2 convolution_subtract_fusion.26
  72.6 0.2 convolution_subtract_fusion.25
  73.0 0.2 convolution_subtract_fusion.24
  73.5 0.2 convolution_subtract_fusion.23
  73.9 0.2 convolution_subtract_fusion.22
  74.4 0.2 convolution_subtract_fusion.21
  75.3 0.2 convolution_subtract_fusion.19
  75.7 0.3 convolution_subtract_fusion.18
  76.6 0.3 convolution_subtract_fusion.16
  77.5 0.3 convolution_subtract_fusion.14
  78.2 0.6 copy-done.4
  79.4 37.0 %all-gather.2.cloned.1.call-done = f32[16,16,1024]{2,1,0:T(8,128)} async-done(((f32[1,16,1024]{2,1,0:T(8,128)}), f32[16,16,1024]{2,1,0:T(8,128)}) %all-gather.2.cloned.1.call-update) | async-done | bytes 1048592 | tf_op jit(solution)/shard_map/all_gather | solution.py:140
  116.5 1.8 gather_fusion
  118.4 0.8 gather_fusion.1
  122.7 1.1 multiply_reduce_fusion.7
  125.4 0.3 collective-permute-start.4
  125.7 0.9 collective-permute-done.4
  126.6 0.6 collective-permute-start.5
  127.2 3.1 %collective-permute-done.5 = f32[2,2,16]{2,1,0:T(2,128)S(1)} collective-permute-done((f32[2,2,16]{2,1,0:T(2,128)S(1)}, f32[2,2,16]{2,1,0:T(2,128)S(1)}, u32[]{:S(2)}, u32[]{:S(2)}) %collective-permute-start.5) | collective-permute-done | bytes 288 | tf_op jit(solution)/shard_map/ppermute | solution.py:25
  130.3 0.6 collective-permute-start.6
  131.0 39.4 %psum.15 = f32[8]{0:T(128)S(1)} all-reduce(f32[8]{0:T(128)S(1)} %reduce_sum.369), channel_id=1, replica_groups=mesh['group'=2,'strip'=16] {'group','strip'}, use_global_device_ids=true, to_apply=%region_38.39 | all-reduce | flops 8 | bytes 64 | tf_op jit(solution)/shard_map/psum | solution.py:134
  170.4 1.4 collective-permute-start.7
  171.8 3.2 %collective-permute-done.7 = f32[8,2,16]{2,1,0:T(2,128)S(1)} collective-permute-done((f32[8,2,16]{2,1,0:T(2,128)S(1)}, f32[8,2,16]{2,1,0:T(2,128)S(1)}, u32[]{:S(2)}, u32[]{:S(2)}) %collective-permute-start.7) | collective-permute-done | bytes 1056 | tf_op jit(solution)/shard_map/ppermute | solution.py:25
  175.1 0.2 fusion.80
  175.5 0.2 convolution_subtract_fusion.13
  175.9 0.2 convolution_subtract_fusion.12
  176.4 0.2 convolution_subtract_fusion.11
  176.8 0.2 convolution_subtract_fusion.10
  177.3 0.2 convolution_subtract_fusion.9
  177.7 0.2 convolution_subtract_fusion.8
  178.2 0.2 convolution_subtract_fusion.7
  178.6 0.2 convolution_subtract_fusion.6
  179.1 0.2 convolution_subtract_fusion.5
  179.5 0.2 convolution_subtract_fusion.4
  182.0 0.6 copy-done.5
  (233 shorter events, 19.4 us)
Async XLA Ops:
  7.2 109.3 %all-gather.2.cloned.1.call-start = ((), (), s32[]{:S(2)}) async-start(), calls=%async_computation | async-start | bytes 1114112 | tf_op jit(solution)/shard_map/all_gather | solution.py:140
  8.3 1.0 copy-start
  14.5 44.3 %copy-start.7 = (s32[1,4]{1,0:T(1,128)S(1)}, s32[1,4]{1,0:T(1,128)}, u32[]{:S(2)}) copy-start(s32[1,4]{1,0:T(1,128)} %param.14) | copy-start | bytes 52
  14.5 44.3 %copy-start.8 = (s32[32,1]{0,1:T(1,128)S(1)}, s32[32,1]{0,1:T(1,128)}, u32[]{:S(2)}) copy-start(s32[32,1]{0,1:T(1,128)} %param.12) | copy-start | bytes 388
  14.6 56.7 %copy-start.6 = (s32[32]{0:T(128)S(1)}, s32[32]{0:T(128)}, u32[]{:S(2)}) copy-start(s32[32]{0:T(128)} %param.13) | copy-start | bytes 388
  14.6 56.9 %copy-start.1 = (f32[1,8,128,128]{3,2,1,0:T(8,128)S(1)}, f32[1,8,128,128]{3,2,1,0:T(8,128)}, u32[]{:S(2)}) copy-start(f32[1,8,128,128]{3,2,1,0:T(8,128)} %param.15) | copy-start | bytes 1572868
  15.0 56.6 %copy-start.2 = (f32[1,7,128,128]{3,2,1,0:T(8,128)S(1)}, f32[1,7,128,128]{3,2,1,0:T(8,128)}, u32[]{:S(2)}) copy-start(f32[1,7,128,128]{3,2,1,0:T(8,128)} %param.16) | copy-start | bytes 1376260
  16.6 42.3 %collective-permute-start = (f32[1,2,16]{2,1,0:T(2,128)S(1)}, f32[1,2,16]{2,1,0:T(2,128)S(1)}, u32[]{:S(2)}, u32[]{:S(2)}) collective-permute-start(f32[1,2,16]{2,1,0:T(2,128)S(1)} %bitcast.594), channel_id=1, source_target_pairs={{0,1},{1,0},{2,3},{3,2},{4,5},{5,4},{6,7},{7,6},{8,9},{9,8},{10,11... | collective-permute-start | bytes 392 | tf_op jit(solution)/shard_map/ppermute | solution.py:25
  59.0 3.9 %collective-permute-start.1 = (f32[2,2,16]{2,1,0:T(2,128)S(1)}, f32[2,2,16]{2,1,0:T(2,128)S(1)}, u32[]{:S(2)}, u32[]{:S(2)}) collective-permute-start(f32[2,2,16]{2,1,0:T(2,128)S(1)} %get-tuple-element.325), channel_id=1, source_target_pairs={{0,2},{1,3},{2,0},{3,1},{4,6},{5,7},{6,4},{7,5},{8,10},{9,11},{10,... | collective-permute-start | bytes 776 | tf_op jit(solution)/shard_map/ppermute | solution.py:25
  62.9 3.7 %collective-permute-start.2 = (f32[4,2,16]{2,1,0:T(2,128)S(1)}, f32[4,2,16]{2,1,0:T(2,128)S(1)}, u32[]{:S(2)}, u32[]{:S(2)}) collective-permute-start(f32[4,2,16]{2,1,0:T(2,128)S(1)} %bitcast.589), channel_id=1, source_target_pairs={{0,4},{1,5},{2,6},{3,7},{4,0},{5,1},{6,2},{7,3},{8,12},{9,13},{10,... | collective-permute-start | bytes 1544 | tf_op jit(solution)/shard_map/ppermute | solution.py:25
  66.6 4.6 %collective-permute-start.3 = (f32[8,2,16]{2,1,0:T(2,128)S(1)}, f32[8,2,16]{2,1,0:T(2,128)S(1)}, u32[]{:S(2)}, u32[]{:S(2)}) collective-permute-start(f32[8,2,16]{2,1,0:T(2,128)S(1)} %bitcast.581), channel_id=1, source_target_pairs={{0,8},{1,9},{2,10},{3,11},{4,12},{5,13},{6,14},{7,15},{8,0},{9,1},... | collective-permute-start | bytes 3080 | tf_op jit(solution)/shard_map/ppermute | solution.py:25
  72.3 2.5 %copy-start.3 = (f32[1,7,128,128]{3,2,1,0:T(8,128)S(1)}, f32[1,7,128,128]{3,2,1,0:T(8,128)}, u32[]{:S(2)}) copy-start(f32[1,7,128,128]{3,2,1,0:T(8,128)} %param.17) | copy-start | bytes 1376260
  78.2 0.6 copy-start.4
  125.4 1.2 collective-permute-start.4
  126.6 3.6 %collective-permute-start.5 = (f32[2,2,16]{2,1,0:T(2,128)S(1)}, f32[2,2,16]{2,1,0:T(2,128)S(1)}, u32[]{:S(2)}, u32[]{:S(2)}) collective-permute-start(f32[2,2,16]{2,1,0:T(2,128)S(1)} %get-tuple-element.323), channel_id=1, source_target_pairs={{0,2},{1,3},{2,0},{3,1},{4,6},{5,7},{6,4},{7,5},{8,10},{9,11},{10,... | collective-permute-start | bytes 776 | tf_op jit(solution)/shard_map/ppermute | solution.py:25
  130.3 40.1 %collective-permute-start.6 = (f32[4,2,16]{2,1,0:T(2,128)S(1)}, f32[4,2,16]{2,1,0:T(2,128)S(1)}, u32[]{:S(2)}, u32[]{:S(2)}) collective-permute-start(f32[4,2,16]{2,1,0:T(2,128)S(1)} %bitcast.587), channel_id=1, source_target_pairs={{0,4},{1,5},{2,6},{3,7},{4,0},{5,1},{6,2},{7,3},{8,12},{9,13},{10,... | collective-permute-start | bytes 1544 | tf_op jit(solution)/shard_map/ppermute | solution.py:25
  170.4 4.6 %collective-permute-start.7 = (f32[8,2,16]{2,1,0:T(2,128)S(1)}, f32[8,2,16]{2,1,0:T(2,128)S(1)}, u32[]{:S(2)}, u32[]{:S(2)}) collective-permute-start(f32[8,2,16]{2,1,0:T(2,128)S(1)} %bitcast.583), channel_id=1, source_target_pairs={{0,8},{1,9},{2,10},{3,11},{4,12},{5,13},{6,14},{7,15},{8,0},{9,1},... | collective-permute-start | bytes 3080 | tf_op jit(solution)/shard_map/ppermute | solution.py:25
  182.0 0.6 copy-start.5
Sparse Core Ops, SparseCore 0:
  79.0 37.4 all-gather.1
